TPU v7x, 512 devices: a whole 4x4x16 slice. The times are simulated.
512 devices in a mesh: dp: 4 (over x), ctx: 16 (over z), mp: 8 (over y, core).
Axes of the slice: x: 4, y: 4, z: 16, core: 2. Of those that a mesh axis runs over, the one named last changes fastest.
Arguments:
- tokens: bfloat16 [4, 2048, 4096], P('dp', 'ctx'), may hold values from -52 to 52
- x_weight: bfloat16 [4096, 8192], P(('dp', 'ctx'), 'mp'), may hold values from -0.09375 to 0.09375
- bc_weight: bfloat16 [4096, 1024], P(('dp', 'ctx'), 'mp'), may hold values from -0.09375 to 0.09375
- dt_weight: bfloat16 [4096, 128], P(('dp', 'ctx'), 'mp'), may hold values from -0.0234375 to 0.0234375
- conv_x: float32 [5, 8192], P(None, 'mp'), may hold values from -0.5 to 0.5
- conv_bc: float32 [5, 1024], P(None, 'mp'), may hold values from -0.5 to 0.5
- dt_bias: float32 [128], P('mp'), may hold values from -4.5 to -2.5
- a_log: float32 [128], P('mp')
- d_skip: float32 [128], P('mp'), may hold values from 0.5 to 1.5
- norm_gain: float32 [8192], P('mp'), may hold values from 0.5 to 1.5
Outputs:
- mixer_out: bfloat16 [4, 2048, 8192], P('dp', 'ctx', 'mp')
- kurtosis: float32 [4096], P('mp')
All inputs are finite; a program needn't handle non-finite values.
Results may differ from a plain program's by a relative error of at most 0.015.
Values may be sent and summed in bfloat16 or wider, within the bound.
No kernel may reach another device: no remote copies, remote signals or barrier semaphores. Data moves between devices by JAX's collectives and lax.ppermute only.
A program may use at most 64 MiB of HBM per device.

v0:
```python
import jax
import jax.numpy as jnp
from jax import lax
from jax.sharding import PartitionSpec as P

ROOT = 64
HEADS = 128
G = 4
NS = 128
HIGH = lax.Precision.HIGHEST


def passed_along(value, axis, steps):
    count = lax.axis_size(axis)
    first, last = (max(0, -steps), min(count, count - steps))
    return lax.ppermute(value, axis, [(source, source + steps) for source in range(first, last)])


def entering(decay, contrib, axis):
    length, place = (lax.axis_size(axis), lax.axis_index(axis))
    lanes = contrib.shape[-1]
    rows = contrib.size // lanes
    tail = jnp.zeros((8, lanes), jnp.float32).at[0, : decay.size].set(decay.reshape(-1))
    flat = jnp.concatenate([contrib.reshape(rows, lanes), tail]).astype(jnp.bfloat16)
    everything = lax.all_gather(flat, axis).astype(jnp.float32)
    states = everything[:, :rows].reshape((length,) + contrib.shape)
    decays = everything[:, rows, : decay.size].reshape((length,) + decay.shape)
    source = lax.broadcasted_iota(jnp.int32, (length, length), 0)
    between = lax.broadcasted_iota(jnp.int32, (length, length), 1)
    inside = jnp.logical_and(between > source, between < place)
    factors = jnp.where(inside[:, :, None, None], decays[None], 1.0)
    weights = jnp.prod(factors, 1)
    weights = jnp.where((source[:, 0] < place)[:, None, None], weights, 0.0)
    return jnp.einsum("jgh,jghpn->ghpn", weights, states, precision=HIGH)


def hadamard_signs(sign_order):
    row_index = lax.broadcasted_iota(jnp.int32, (sign_order, sign_order), 0)
    col_index = lax.broadcasted_iota(jnp.int32, (sign_order, sign_order), 1)
    common = jnp.bitwise_and(row_index, col_index)
    parity = jnp.zeros((sign_order, sign_order), jnp.int32)
    for bit_index in range(sign_order.bit_length() - 1):
        parity = parity + jnp.bitwise_and(jnp.right_shift(common, bit_index), 1)
    return 1.0 - 2.0 * jnp.bitwise_and(parity, 1).astype(jnp.float32)


def kurtosis_from(powers, row_count):
    average = powers[0] / row_count
    second = powers[1] / row_count - average * average
    fourth = (
        powers[3] / row_count
        - 4.0 * average * powers[2] / row_count
        + 6.0 * average * average * powers[1] / row_count
        - 3.0 * average * average * average * average
    )
    return fourth / (second * second + 1e-06)


def shards(
    tokens, x_weight, bc_weight, dt_weight, conv_x, conv_bc, dt_bias, a_log, d_skip, norm_gain
):
    tok_rows = tokens.shape[1]
    model_width = tokens.shape[2]
    signs = hadamard_signs(ROOT)
    blocks = tokens.reshape(tok_rows, ROOT, ROOT)
    first_pass = jnp.einsum(
        "tab,ac->tcb", blocks, signs.astype(jnp.bfloat16), preferred_element_type=jnp.float32
    )
    second = jnp.einsum("tcb,bd->tcd", first_pass, signs, precision=HIGH)
    rotated = (second.reshape(tok_rows, model_width) / ROOT).astype(jnp.bfloat16)
    channel_share = model_width // lax.axis_size("mp")
    own_cols = lax.dynamic_slice_in_dim(
        rotated, lax.axis_index("mp") * channel_share, channel_share, 1
    ).astype(jnp.float32)
    square = own_cols * own_cols
    powers = jnp.stack(
        [
            jnp.sum(own_cols, 0),
            jnp.sum(square, 0),
            jnp.sum(square * own_cols, 0),
            jnp.sum(square * square, 0),
        ]
    )
    row_count = float(tok_rows * lax.axis_size("dp") * lax.axis_size("ctx"))
    totals = lax.psum(lax.psum(powers, "ctx"), "dp")
    totals, rotated = lax.optimization_barrier((totals, rotated))
    kurtosis = kurtosis_from(totals, row_count)
    local_panel = jnp.concatenate([x_weight, bc_weight, dt_weight], 1)
    panel = lax.all_gather(local_panel, ("dp", "ctx"), axis=0, tiled=True)
    both = jnp.dot(rotated, panel, preferred_element_type=jnp.float32)
    x_end = x_weight.shape[1]
    bc_end = x_end + bc_weight.shape[1]
    projected = (both[:, :x_end], both[:, x_end:bc_end], both[:, bc_end:])
    x_cols = x_weight.shape[1]
    joined = jnp.concatenate(
        [projected[0].astype(jnp.bfloat16), projected[1].astype(jnp.bfloat16)], 1
    )
    dt_proj = lax.optimization_barrier(projected[2].astype(jnp.bfloat16))
    conv_taps = jnp.concatenate([conv_x, conv_bc], 1)
    kernel = conv_taps.shape[0] - 1
    rim_rows = passed_along(joined[tok_rows - (kernel - 1) :], "ctx", 1)
    padded = jnp.concatenate([rim_rows, joined], 0)
    conv_sum = conv_taps[kernel]
    for tap_index in range(kernel):
        conv_sum = conv_sum + conv_taps[tap_index] * padded[tap_index : tap_index + tok_rows]
    convolved = jax.nn.silu(conv_sum).astype(jnp.bfloat16)
    x_conv = convolved[:, :x_cols]
    group_all = lax.all_gather(convolved[:, x_cols:], "mp", axis=1, tiled=True)
    heads_dev = dt_weight.shape[1]
    head_size = x_cols // heads_dev
    per_group = HEADS // G
    groups_here = max(1, heads_dev // per_group)
    heads_local = heads_dev // groups_here
    first_group = lax.axis_index("mp") * heads_dev // per_group
    write_all = group_all[:, : G * NS].reshape(tok_rows, G, NS)
    read_all = group_all[:, G * NS :].reshape(tok_rows, G, NS)
    write_here = lax.dynamic_slice_in_dim(write_all, first_group, groups_here, 1)
    read_here = lax.dynamic_slice_in_dim(read_all, first_group, groups_here, 1)
    step_size = jax.nn.softplus(dt_proj.astype(jnp.float32) + dt_bias)
    decay_rate = step_size * jnp.exp(a_log)
    cumulative = jnp.cumsum(decay_rate, 0)
    block_end = cumulative[-1]
    causal = lax.broadcasted_iota(jnp.int32, (tok_rows, tok_rows), 0) >= lax.broadcasted_iota(
        jnp.int32, (tok_rows, tok_rows), 1
    )
    spread = cumulative.T[:, :, None] - cumulative.T[:, None, :]
    decay_mask = jnp.where(causal, jnp.exp(-jnp.where(causal, spread, 0.0)), 0.0)
    scores = jnp.einsum("tgn,sgn->gts", read_here, write_here, preferred_element_type=jnp.float32)
    weights = (
        scores[:, None]
        * decay_mask.reshape(groups_here, heads_local, tok_rows, tok_rows)
        * step_size.T.reshape(groups_here, heads_local, 1, tok_rows)
    ).astype(jnp.bfloat16)
    x_heads = x_conv.reshape(tok_rows, groups_here, heads_local, head_size)
    within_block = jnp.einsum(
        "ghts,sghp->tghp", weights, x_heads, preferred_element_type=jnp.float32
    )
    update = (
        (jnp.exp(-(block_end - cumulative)) * step_size).reshape(
            tok_rows, groups_here, heads_local
        )[..., None]
        * x_heads
    ).astype(jnp.bfloat16)
    contrib = jnp.einsum("sghp,sgn->ghpn", update, write_here, preferred_element_type=jnp.float32)
    carried = entering(jnp.exp(-block_end).reshape(groups_here, heads_local), contrib, "ctx")
    from_before = jnp.exp(-cumulative).reshape(tok_rows, groups_here, heads_local)[
        ..., None
    ] * jnp.einsum("tgn,ghpn->tghp", read_here.astype(jnp.float32), carried, precision=HIGH)
    output_raw = (
        within_block
        + from_before
        + d_skip.reshape(groups_here, heads_local)[None, :, :, None] * x_heads.astype(jnp.float32)
    )
    mean_square = jnp.mean(output_raw * output_raw, -1, keepdims=True)
    normed = (
        output_raw
        * lax.rsqrt(mean_square + 1e-05)
        * norm_gain.reshape(groups_here, heads_local, head_size)
    )
    return (normed.reshape(1, tok_rows, x_cols).astype(jnp.bfloat16), kurtosis)


def solution(mesh):
    return jax.shard_map(
        shards,
        mesh=mesh,
        in_specs=(
            P("dp", "ctx", None),
            P(("dp", "ctx"), "mp"),
            P(("dp", "ctx"), "mp"),
            P(("dp", "ctx"), "mp"),
            P(None, "mp"),
            P(None, "mp"),
            P("mp"),
            P("mp"),
            P("mp"),
            P("mp"),
        ),
        out_specs=(P("dp", "ctx", "mp"), P("mp")),
        check_vma=False,
    )
```

profile of v0, /device:TPU:4, one launch (start us, length us, event | category | flops | bytes accessed | tf_op | source)
XLA Modules:
  0.0 302.1 jit_solution(1857820000837005802)
XLA Ops:
  7.2 0.0 all-gather.3.cloned.1.call-start
  7.2 0.8 copy.43
  8.0 1.6 pad_maximum_fusion.1
  9.6 0.0 all-gather.3.cloned.1.call-update
  9.6 0.0 all-gather.5.cloned.1.call-start
  9.7 0.0 copy-start.5
  9.7 0.0 copy-start.1
  9.7 0.0 copy-start.3
  9.7 1.6 copy.40
  11.3 0.9 convolution_bitcast_fusion
  12.2 3.3 %multiply_convert_fusion = bf16[128,64,64]{0,2,1:T(8,128)(2,1)S(1)} fusion(f32[128,64,64]{0,1,2:T(8,128)S(1)} %convolution_bitcast_fusion), kind=kOutput, calls=%fused_computation.5 | convolution fusion | flops 403791872 | bytes 3145728 | tf_op jit(solution)/shard_map/tcb,bd->tcd/dot_general | solution.py:69
  15.6 0.3 convert_reduce_fusion
  15.9 37.2 %psum.14 = f32[4,512]{1,0:T(4,128)S(1)} all-reduce(f32[4,512]{1,0:T(4,128)S(1)} %pad_maximum_fusion.2), channel_id=1, replica_groups=mesh['dp'=4,'ctx'=16,'mp'=8] {'ctx'}, use_global_device_ids=true, to_apply=%region_4.0 | all-reduce | flops 2048 | bytes 16384 | tf_op jit(solution)/shard_map/psum | solution.py:85
  53.1 8.4 %psum.15 = f32[4,512]{1,0:T(4,128)S(1)} all-reduce(f32[4,512]{1,0:T(4,128)S(1)} %psum.14), channel_id=1, replica_groups=mesh['dp'=4,'ctx'=16,'mp'=8] {'dp'}, use_global_device_ids=true, to_apply=%region_5.0 | all-reduce | flops 2048 | bytes 16384 | tf_op jit(solution)/shard_map/psum | solution.py:85
  61.5 0.0 copy-done.5
  61.5 0.0 copy-done.1
  61.6 0.0 copy-done.3
  61.6 0.1 slice_reduce_fusion.4
  61.7 0.0 copy-start.4
  61.7 116.0 %all-gather.3.cloned.1.call-done = bf16[4096,1168]{1,0:T(8,128)(2,1)} async-done(((bf16[64,1168]{1,0:T(8,128)(2,1)}), bf16[4096,1168]{1,0:T(8,128)(2,1)}) %all-gather.3.cloned.1.call-update) | async-done | bytes 9568272 | tf_op jit(solution)/shard_map/all_gather | solution.py:89
  177.7 8.0 %convolution_convert_fusion = bf16[128,1168]{0,1:T(8,128)(2,1)S(1)} fusion(bf16[128,4096]{0,1:T(8,128)(2,1)S(1)} %bitcast.81, bf16[4096,1168]{1,0:T(8,128)(2,1)} %all-gather.3.cloned.1.call-done), kind=kOutput, calls=%fused_computation.2 | convolution fusion | flops 1224886272 | bytes 10915840 | tf_op jit(solution)/shard_map/dot_general | solution.py:90
  185.7 0.0 copy-start.2
  185.7 0.1 slice.121
  185.9 0.0 copy-done.4
  185.9 0.1 broadcast_multiply_fusion
  186.0 0.1 copy.45
  186.1 0.2 reduce_window_sum.11
  186.2 0.1 copy.49
  186.3 3.3 %collective-permute-start = (bf16[3,1152]{0,1:T(8,128)(2,1)S(1)}, bf16[3,1152]{0,1:T(8,128)(2,1)S(1)}, u32[]{:S(2)}, u32[]{:S(2)}) collective-permute-start(bf16[3,1152]{0,1:T(8,128)(2,1)S(1)} %slice.121), channel_id=1, source_target_pairs={{0,8},{8,16},{16,24},{24,32},{32,40},{40,48},{48,56},{56,64},{64,7... | collective-permute-start | bytes 20744 | tf_op jit(solution)/shard_map/ppermute | solution.py:16
  189.6 0.1 fusion.60
  189.7 4.1 %collective-permute-done = bf16[3,1152]{0,1:T(8,128)(2,1)S(1)} collective-permute-done((bf16[3,1152]{0,1:T(8,128)(2,1)S(1)}, bf16[3,1152]{0,1:T(8,128)(2,1)S(1)}, u32[]{:S(2)}, u32[]{:S(2)}) %collective-permute-start) | collective-permute-done | bytes 6944 | tf_op jit(solution)/shard_map/ppermute | solution.py:16
  193.8 1.4 multiply_convert_fusion.2
  195.2 0.0 copy-start
  195.2 13.4 %all_gather.11 = bf16[128,1024]{0,1:T(8,128)(2,1)S(1)} all-gather(bf16[128,128]{0,1:T(8,128)(2,1)S(1)} %slice.131), channel_id=1, replica_groups=mesh['dp'=4,'ctx'=16,'mp'=8] {'mp'}, dimensions={1}, use_global_device_ids=true | all-gather | bytes 294912 | tf_op jit(solution)/shard_map/all_gather | solution.py:108
  208.6 0.1 multiply_convert_fusion.5
  208.7 0.2 fusion.9
  208.9 0.7 fusion.22
  209.7 0.0 all-gather.5.cloned.1.call-update
  209.7 0.0 copy-done.2
  209.7 0.1 mul.242
  209.8 0.6 fusion.39
  210.5 0.1 copy.48
  210.5 0.1 copy.46
  210.6 0.2 fusion.26
  210.8 75.6 %all-gather.5.cloned.1.call-done = bf16[16,1032,128]{2,1,0:T(8,128)(2,1)} async-done(((bf16[1,1032,128]{2,1,0:T(8,128)(2,1)}), bf16[16,1032,128]{2,1,0:T(8,128)(2,1)}) %all-gather.5.cloned.1.call-update) | async-done | bytes 4227088 | tf_op jit(solution)/shard_map/all_gather | solution.py:25
  286.3 0.8 slice_convert_fusion
  287.1 0.1 select_reduce_fusion
  287.2 0.1 select_bitcast_fusion
  287.3 0.1 copy.51
  287.4 0.0 slice-start
  287.4 0.0 copy-done
  287.4 0.0 copy-start.6
  287.4 2.2 slice-done
  289.6 0.0 slice-start.1
  289.6 3.6 %fusion = f32[16,1,64,128]{3,1,2,0:T(1,128)S(1)} fusion(f32[16,16,1,1]{0,2,3,1:T(1,128)S(1)} %copy.51, bf16[16,16,64,128]{3,2,1,0:T(8,128)(2,1)S(1)} %bitcast.79), kind=kOutput, calls=%fused_computation | convolution fusion | flops 25165824 | bytes 4719616 | tf_op jit(solution)/shard_map/jgh,jghpn->ghpn/dot_general | solution.py:34
  293.1 0.4 fusion.8
  293.5 0.0 copy-done.6
  293.5 0.0 slice-done.1
  293.5 0.6 multiply_reduce_fusion
  294.2 0.2 multiply_convert_fusion.4
  294.4 0.9 copy.50
  (16 shorter events, 0.2 us)
Async XLA Ops:
  7.2 170.5 %all-gather.3.cloned.1.call-start = ((), (), s32[]{:S(2)}) async-start(), calls=%async_computation | async-start | bytes 10649600 | tf_op jit(solution)/shard_map/all_gather | solution.py:89
  9.6 276.7 %all-gather.5.cloned.1.call-start = ((), (), s32[]{:S(2)}) async-start(), calls=%async_computation.1 | async-start | bytes 4491264 | tf_op jit(solution)/shard_map/all_gather | solution.py:25
  9.7 51.8 %copy-start.5 = (f32[16]{0:T(128)S(1)}, f32[16]{0:T(128)}, u32[]{:S(2)}) copy-start(f32[16]{0:T(128)} %param.19) | copy-start | bytes 196
  9.7 51.9 %copy-start.1 = (f32[5,1024]{1,0:T(8,128)S(1)}, f32[5,1024]{1,0:T(8,128)}, u32[]{:S(2)}) copy-start(f32[5,1024]{1,0:T(8,128)} %param.16) | copy-start | bytes 61444
  9.7 51.9 %copy-start.3 = (f32[5,128]{1,0:T(8,128)S(1)}, f32[5,128]{1,0:T(8,128)}, u32[]{:S(2)}) copy-start(f32[5,128]{1,0:T(8,128)} %param.17) | copy-start | bytes 7684
  61.7 124.2 %copy-start.4 = (f32[16]{0:T(128)S(1)}, f32[16]{0:T(128)}, u32[]{:S(2)}) copy-start(f32[16]{0:T(128)} %param.18) | copy-start | bytes 196
  185.7 24.0 %copy-start.2 = (f32[1024]{0:T(1024)S(1)}, f32[1024]{0:T(1024)}, u32[]{:S(2)}) copy-start(f32[1024]{0:T(1024)} %param.21) | copy-start | bytes 12292
  186.3 7.5 %collective-permute-start = (bf16[3,1152]{0,1:T(8,128)(2,1)S(1)}, bf16[3,1152]{0,1:T(8,128)(2,1)S(1)}, u32[]{:S(2)}, u32[]{:S(2)}) collective-permute-start(bf16[3,1152]{0,1:T(8,128)(2,1)S(1)} %slice.121), channel_id=1, source_target_pairs={{0,8},{8,16},{16,24},{24,32},{32,40},{40,48},{48,56},{56,64},{64,7... | collective-permute-start | bytes 20744 | tf_op jit(solution)/shard_map/ppermute | solution.py:16
  195.2 92.2 %copy-start = (bf16[128,1152]{0,1:T(8,128)(2,1)}, bf16[128,1152]{0,1:T(8,128)(2,1)S(1)}, u32[]{:S(2)}) copy-start(bf16[128,1152]{0,1:T(8,128)(2,1)S(1)} %multiply_convert_fusion.2) | copy-start | bytes 884740
  287.4 2.2 slice-start
  287.4 6.1 %copy-start.6 = (f32[16]{0:T(128)S(1)}, f32[16]{0:T(128)}, u32[]{:S(2)}) copy-start(f32[16]{0:T(128)} %param.20) | copy-start | bytes 196
  289.6 4.0 %slice-start.1 = ((bf16[128,1152]{0,1:T(8,128)(2,1)}), bf16[128,1024]{0,1:T(8,128)(2,1)S(1)}, s32[]{:S(2)}) async-start(bf16[128,1152]{0,1:T(8,128)(2,1)} %copy-done), calls=%async_computation.3 | async-start | bytes 524288 | tf_op jit(solution)/shard_map/slice | solution.py:107
Sparse Core Ops, SparseCore 0:
  11.5 166.0 all-gather.2
  209.8 76.4 all-gather.4
where the time goes:
time: 302 us
  waiting for transfers between devices  196 us (65%)
  blocking collectives  58.9 us (20%)
  matrix products  17.2 us (6%)
  between operations  14.4 us (5%)
  other arithmetic  6.37 us (2%)
  local copies, waits for them, and re-layouts  6.17 us (2%)
  starting transfers between devices  3.33 us (1%)
    all_gather x1, waiting for transfers between devices, shards(): panel = lax.all_gather(local_panel, ('dp', 'ctx'), axis=0, tiled=True)  116 us
    all_gather x1, waiting for transfers between devices, entering(): everything = lax.all_gather(flat, axis).astype(jnp.float32)  75.6 us
    psum x2, blocking collectives, shards(): totals = lax.psum(lax.psum(powers, 'ctx'), 'dp')  45.6 us
    all_gather x1, blocking collectives, shards(): group_all = lax.all_gather(convolved[:, x_cols:], 'mp', axis=1, tiled=True)  13.4 us
    dot_general x1, matrix products, shards(): both = jnp.dot(rotated, panel, preferred_element_type=jnp.float32)  8.01 us
  transfers between devices with their start and end apart: 3, of which 3 were waited for; matrix products, arithmetic and copies ran while one was open for 2% of the time, Pallas kernels for 0%

commit v1 on v0

--- a/solution.py
+++ b/solution.py
@@ -8,6 +8,28 @@
 G = 4
 NS = 128
 HIGH = lax.Precision.HIGHEST
+
+
+def in_order(blocks, dim):
+    shape = list(blocks.shape[1:])
+    shape[dim] *= blocks.shape[0]
+    return jnp.moveaxis(blocks, 0, dim).reshape(shape)
+
+
+def ring_gather(x, axis, dim):
+    devices = lax.axis_size(axis)
+    pairs = [(i, (i + 1) % devices) for i in range(devices)]
+    back = [(b, a) for a, b in pairs]
+    lower, upper = ([], [])
+    for hop in range(devices - 1):
+        if hop % 2 == 0:
+            lower.append(lax.ppermute(lower[-1] if lower else x, axis, pairs))
+        else:
+            upper.append(lax.ppermute(upper[-1] if upper else x, axis, back))
+    blocks = jnp.stack([*lower[::-1], x, *upper])
+    shift = lax.axis_index(axis) - len(lower)
+    blocks = blocks[(jnp.arange(devices) - shift) % devices]
+    return in_order(blocks, dim)
 
 
 def passed_along(value, axis, steps):
@@ -105,7 +127,7 @@
         conv_sum = conv_sum + conv_taps[tap_index] * padded[tap_index : tap_index + tok_rows]
     convolved = jax.nn.silu(conv_sum).astype(jnp.bfloat16)
     x_conv = convolved[:, :x_cols]
-    group_all = lax.all_gather(convolved[:, x_cols:], "mp", axis=1, tiled=True)
+    group_all = ring_gather(convolved[:, x_cols:], "mp", 1)
     heads_dev = dt_weight.shape[1]
     head_size = x_cols // heads_dev
     per_group = HEADS // G

time: 302 us -> 308 us (1.020)
  blocking collectives: 58.9 us -> 45.6 us
  starting transfers between devices: 3.33 us -> 12.4 us
  waiting for transfers between devices: 196 us -> 205 us
    all_gather x1 -> x0, blocking collectives: 13.4 us -> none  [shards(): group_all = lax.all_gather(convolved[:, x_cols:], 'mp', axis=1, tiled=True)]
    ppermute x0 -> x7, starting transfers between devices: none -> 8.92 us  [the longest x3 8.89 us: ring_gather(): upper.append(lax.ppermute(upper[-1] if upper else x, axis, back))]
    ppermute x0 -> x7, waiting for transfers between devices: none -> 8.71 us  [the longest x4 8.63 us: ring_gather(): lower.append(lax.ppermute(lower[-1] if lower else x, axis, pairs))]
  transfers between devices with their start and end apart: 3 -> 10, of which waited for: 3 -> 7; matrix products, arithmetic and copies ran while one was open for 2% -> 3% of each run, Pallas kernels for 0% -> 0%
where the time goes in v1:
time: 308 us
  waiting for transfers between devices  205 us (67%)
  blocking collectives  45.6 us (15%)
  matrix products  17.2 us (6%)
  between operations  14.5 us (5%)
  starting transfers between devices  12.4 us (4%)
  local copies, waits for them, and re-layouts  6.83 us (2%)
  other arithmetic  6.39 us (2%)
    all_gather x1, waiting for transfers between devices, shards(): panel = lax.all_gather(local_panel, ('dp', 'ctx'), axis=0, tiled=True)  116 us
    all_gather x1, waiting for transfers between devices, entering(): everything = lax.all_gather(flat, axis).astype(jnp.float32)  76.1 us
    psum x2, blocking collectives, shards(): totals = lax.psum(lax.psum(powers, 'ctx'), 'dp')  45.6 us
    ppermute x3, starting transfers between devices, ring_gather(): upper.append(lax.ppermute(upper[-1] if upper else x, axis, back))  8.89 us
    ppermute x4, waiting for transfers between devices, ring_gather(): lower.append(lax.ppermute(lower[-1] if lower else x, axis, pairs))  8.63 us
    dot_general x1, matrix products, shards(): both = jnp.dot(rotated, panel, preferred_element_type=jnp.float32)  8.01 us
  transfers between devices with their start and end apart: 10, of which 7 were waited for; matrix products, arithmetic and copies ran while one was open for 3% of the time, Pallas kernels for 0%

profile of v1, /device:TPU:4, one launch (start us, length us, event | category | flops | bytes accessed | tf_op | source)
XLA Modules:
  0.0 307.7 jit_solution(195308883103428076)
XLA Ops:
  7.2 0.0 all-gather.3.cloned.1.call-start
  7.2 0.8 copy.43
  8.0 1.6 pad_maximum_fusion.1
  9.6 0.0 all-gather.3.cloned.1.call-update
  9.6 0.0 all-gather.5.cloned.1.call-start
  9.7 0.0 copy-start.1
  9.7 0.0 copy-start.3
  9.7 1.6 copy.40
  11.3 0.9 convolution_bitcast_fusion
  12.2 3.3 %multiply_convert_fusion = bf16[128,64,64]{0,2,1:T(8,128)(2,1)S(1)} fusion(f32[128,64,64]{0,1,2:T(8,128)S(1)} %convolution_bitcast_fusion), kind=kOutput, calls=%fused_computation.6 | convolution fusion | flops 403791872 | bytes 3145728 | tf_op jit(solution)/shard_map/tcb,bd->tcd/dot_general | solution.py:91
  15.5 0.3 convert_reduce_fusion
  15.9 37.2 %psum.14 = f32[4,512]{1,0:T(4,128)S(1)} all-reduce(f32[4,512]{1,0:T(4,128)S(1)} %pad_maximum_fusion.2), channel_id=1, replica_groups=mesh['dp'=4,'ctx'=16,'mp'=8] {'ctx'}, use_global_device_ids=true, to_apply=%region_4.0 | all-reduce | flops 2048 | bytes 16384 | tf_op jit(solution)/shard_map/psum | solution.py:107
  53.1 8.4 %psum.15 = f32[4,512]{1,0:T(4,128)S(1)} all-reduce(f32[4,512]{1,0:T(4,128)S(1)} %psum.14), channel_id=1, replica_groups=mesh['dp'=4,'ctx'=16,'mp'=8] {'dp'}, use_global_device_ids=true, to_apply=%region_5.0 | all-reduce | flops 2048 | bytes 16384 | tf_op jit(solution)/shard_map/psum | solution.py:107
  61.5 0.1 slice_reduce_fusion.4
  61.6 0.0 copy-start.5
  61.6 0.0 copy-start.4
  61.6 116.0 %all-gather.3.cloned.1.call-done = bf16[4096,1168]{1,0:T(8,128)(2,1)} async-done(((bf16[64,1168]{1,0:T(8,128)(2,1)}), bf16[4096,1168]{1,0:T(8,128)(2,1)}) %all-gather.3.cloned.1.call-update) | async-done | bytes 9568272 | tf_op jit(solution)/shard_map/all_gather | solution.py:111
  177.7 8.0 %convolution_convert_fusion = bf16[128,1168]{0,1:T(8,128)(2,1)S(1)} fusion(bf16[128,4096]{0,1:T(8,128)(2,1)S(1)} %bitcast.102, bf16[4096,1168]{1,0:T(8,128)(2,1)} %all-gather.3.cloned.1.call-done), kind=kOutput, calls=%fused_computation.3 | convolution fusion | flops 1224886272 | bytes 10915840 | tf_op jit(solution)/shard_map/dot_general | solution.py:112
  185.7 0.0 copy-start.2
  185.7 0.1 slice.123
  185.8 3.4 %collective-permute-start = (bf16[3,1152]{0,1:T(8,128)(2,1)S(1)}, bf16[3,1152]{0,1:T(8,128)(2,1)S(1)}, u32[]{:S(2)}, u32[]{:S(2)}) collective-permute-start(bf16[3,1152]{0,1:T(8,128)(2,1)S(1)} %slice.123), channel_id=1, source_target_pairs={{0,8},{8,16},{16,24},{24,32},{32,40},{40,48},{48,56},{56,64},{64,7... | collective-permute-start | bytes 20744 | tf_op jit(solution)/shard_map/ppermute | solution.py:38
  189.3 0.0 copy-done.5
  189.4 3.9 %collective-permute-done = bf16[3,1152]{0,1:T(8,128)(2,1)S(1)} collective-permute-done((bf16[3,1152]{0,1:T(8,128)(2,1)S(1)}, bf16[3,1152]{0,1:T(8,128)(2,1)S(1)}, u32[]{:S(2)}, u32[]{:S(2)}) %collective-permute-start) | collective-permute-done | bytes 6944 | tf_op jit(solution)/shard_map/ppermute | solution.py:38
  193.3 1.4 multiply_convert_fusion.2
  194.8 0.0 collective-permute-start.1
  194.8 0.1 broadcast_multiply_fusion
  194.9 0.1 copy.45
  195.0 0.2 reduce_window_sum.11
  195.2 4.2 %collective-permute-done.1 = bf16[128,128]{0,1:T(8,128)(2,1)S(1)} collective-permute-done((bf16[128,128]{0,1:T(8,128)(2,1)S(1)}, bf16[128,128]{0,1:T(8,128)(2,1)S(1)}, u32[]{:S(2)}, u32[]{:S(2)}) %collective-permute-start.1) | collective-permute-done | bytes 32800 | tf_op jit(solution)/shard_map/ppermute | solution.py:26
  199.3 0.0 collective-permute-start.2
  199.3 0.1 copy.49
  199.4 3.0 collective-permute-start.5
  202.4 1.5 collective-permute-done.2
  203.9 0.0 collective-permute-start.3
  203.9 0.1 fusion.62
  204.0 0.0 collective-permute-done.5
  204.0 3.0 collective-permute-start.6
  207.0 1.5 collective-permute-done.3
  208.4 0.0 collective-permute-start.4
  208.4 0.1 multiply_convert_fusion.5
  208.5 0.0 collective-permute-done.6
  208.6 3.0 collective-permute-start.7
  211.5 1.5 collective-permute-done.4
  213.1 0.0 collective-permute-done.7
  213.1 0.6 gather_fusion
  213.7 0.2 fusion.9
  214.0 0.7 fusion.22
  214.7 0.0 all-gather.5.cloned.1.call-update
  214.8 0.1 mul.242
  214.9 0.6 fusion.39
  215.5 0.1 copy.48
  215.6 0.1 copy.46
  215.6 0.2 fusion.26
  215.8 76.1 %all-gather.5.cloned.1.call-done = bf16[16,1032,128]{2,1,0:T(8,128)(2,1)} async-done(((bf16[1,1032,128]{2,1,0:T(8,128)(2,1)}), bf16[16,1032,128]{2,1,0:T(8,128)(2,1)}) %all-gather.5.cloned.1.call-update) | async-done | bytes 4227088 | tf_op jit(solution)/shard_map/all_gather | solution.py:47
  292.0 0.8 slice_convert_fusion
  292.7 0.1 select_reduce_fusion
  292.9 0.1 select_bitcast_fusion
  292.9 0.1 copy.51
  293.0 2.2 slice-done
  295.2 3.6 %fusion = f32[16,1,64,128]{3,1,2,0:T(1,128)S(1)} fusion(f32[16,16,1,1]{0,2,3,1:T(1,128)S(1)} %copy.51, bf16[16,16,64,128]{3,2,1,0:T(8,128)(2,1)S(1)} %bitcast.100), kind=kOutput, calls=%fused_computation.1 | convolution fusion | flops 25165824 | bytes 4719616 | tf_op jit(solution)/shard_map/jgh,jghpn->ghpn/dot_general | solution.py:56
  298.8 0.4 fusion.8
  299.1 0.6 multiply_reduce_fusion
  299.8 0.2 multiply_convert_fusion.4
  300.0 0.9 copy.50
  (37 shorter events, 0.3 us)
Async XLA Ops:
  7.2 170.5 %all-gather.3.cloned.1.call-start = ((), (), s32[]{:S(2)}) async-start(), calls=%async_computation | async-start | bytes 10649600 | tf_op jit(solution)/shard_map/all_gather | solution.py:111
  9.6 282.3 %all-gather.5.cloned.1.call-start = ((), (), s32[]{:S(2)}) async-start(), calls=%async_computation.1 | async-start | bytes 4491264 | tf_op jit(solution)/shard_map/all_gather | solution.py:47
  9.7 51.8 %copy-start.1 = (f32[5,1024]{1,0:T(8,128)S(1)}, f32[5,1024]{1,0:T(8,128)}, u32[]{:S(2)}) copy-start(f32[5,1024]{1,0:T(8,128)} %param.16) | copy-start | bytes 61444
  9.7 51.8 %copy-start.3 = (f32[5,128]{1,0:T(8,128)S(1)}, f32[5,128]{1,0:T(8,128)}, u32[]{:S(2)}) copy-start(f32[5,128]{1,0:T(8,128)} %param.17) | copy-start | bytes 7684
  61.6 127.7 %copy-start.5 = (f32[16]{0:T(128)S(1)}, f32[16]{0:T(128)}, u32[]{:S(2)}) copy-start(f32[16]{0:T(128)} %param.19) | copy-start | bytes 196
  61.6 133.2 %copy-start.4 = (f32[16]{0:T(128)S(1)}, f32[16]{0:T(128)}, u32[]{:S(2)}) copy-start(f32[16]{0:T(128)} %param.18) | copy-start | bytes 196
  185.7 29.1 %copy-start.2 = (f32[1024]{0:T(1024)S(1)}, f32[1024]{0:T(1024)}, u32[]{:S(2)}) copy-start(f32[1024]{0:T(1024)} %param.21) | copy-start | bytes 12292
  185.8 7.5 %collective-permute-start = (bf16[3,1152]{0,1:T(8,128)(2,1)S(1)}, bf16[3,1152]{0,1:T(8,128)(2,1)S(1)}, u32[]{:S(2)}, u32[]{:S(2)}) collective-permute-start(bf16[3,1152]{0,1:T(8,128)(2,1)S(1)} %slice.123), channel_id=1, source_target_pairs={{0,8},{8,16},{16,24},{24,32},{32,40},{40,48},{48,56},{56,64},{64,7... | collective-permute-start | bytes 20744 | tf_op jit(solution)/shard_map/ppermute | solution.py:38
  194.7 98.3 %copy-start = (bf16[128,1152]{0,1:T(8,128)(2,1)}, bf16[128,1152]{0,1:T(8,128)(2,1)S(1)}, u32[]{:S(2)}) copy-start(bf16[128,1152]{0,1:T(8,128)(2,1)S(1)} %multiply_convert_fusion.2) | copy-start | bytes 884740
  194.8 4.6 %collective-permute-start.1 = (bf16[128,128]{0,1:T(8,128)(2,1)S(1)}, bf16[128,128]{0,1:T(8,128)(2,1)S(1)}, u32[]{:S(2)}, u32[]{:S(2)}) collective-permute-start(bf16[128,128]{0,1:T(8,128)(2,1)S(1)} %slice.133), channel_id=1, source_target_pairs={{0,1},{1,2},{2,3},{3,4},{4,5},{5,6},{6,7},{7,0},{8,9},{9,10},{10,1... | collective-permute-start | bytes 98312 | tf_op jit(solution)/shard_map/ppermute | solution.py:26
  199.3 4.6 %collective-permute-start.2 = (bf16[128,128]{0,1:T(8,128)(2,1)S(1)}, bf16[128,128]{0,1:T(8,128)(2,1)S(1)}, u32[]{:S(2)}, u32[]{:S(2)}) collective-permute-start(bf16[128,128]{0,1:T(8,128)(2,1)S(1)} %collective-permute-done.1), channel_id=1, source_target_pairs={{0,1},{1,2},{2,3},{3,4},{4,5},{5,6},{6,7},{7,0},{8,9},{9,10},{10,1... | collective-permute-start | bytes 98312 | tf_op jit(solution)/shard_map/ppermute | solution.py:26
  199.4 4.6 %collective-permute-start.5 = (bf16[128,128]{0,1:T(8,128)(2,1)S(1)}, bf16[128,128]{0,1:T(8,128)(2,1)S(1)}, u32[]{:S(2)}, u32[]{:S(2)}) collective-permute-start(bf16[128,128]{0,1:T(8,128)(2,1)S(1)} %slice.133), channel_id=1, source_target_pairs={{1,0},{2,1},{3,2},{4,3},{5,4},{6,5},{7,6},{0,7},{9,8},{10,9},{11,1... | collective-permute-start | bytes 98312 | tf_op jit(solution)/shard_map/ppermute | solution.py:28
  203.9 4.6 %collective-permute-start.3 = (bf16[128,128]{0,1:T(8,128)(2,1)S(1)}, bf16[128,128]{0,1:T(8,128)(2,1)S(1)}, u32[]{:S(2)}, u32[]{:S(2)}) collective-permute-start(bf16[128,128]{0,1:T(8,128)(2,1)S(1)} %collective-permute-done.2), channel_id=1, source_target_pairs={{0,1},{1,2},{2,3},{3,4},{4,5},{5,6},{6,7},{7,0},{8,9},{9,10},{10,1... | collective-permute-start | bytes 98312 | tf_op jit(solution)/shard_map/ppermute | solution.py:26
  204.0 4.6 %collective-permute-start.6 = (bf16[128,128]{0,1:T(8,128)(2,1)S(1)}, bf16[128,128]{0,1:T(8,128)(2,1)S(1)}, u32[]{:S(2)}, u32[]{:S(2)}) collective-permute-start(bf16[128,128]{0,1:T(8,128)(2,1)S(1)} %collective-permute-done.5), channel_id=1, source_target_pairs={{1,0},{2,1},{3,2},{4,3},{5,4},{6,5},{7,6},{0,7},{9,8},{10,9},{11,1... | collective-permute-start | bytes 98312 | tf_op jit(solution)/shard_map/ppermute | solution.py:28
  208.4 4.6 %collective-permute-start.4 = (bf16[128,128]{0,1:T(8,128)(2,1)S(1)}, bf16[128,128]{0,1:T(8,128)(2,1)S(1)}, u32[]{:S(2)}, u32[]{:S(2)}) collective-permute-start(bf16[128,128]{0,1:T(8,128)(2,1)S(1)} %collective-permute-done.3), channel_id=1, source_target_pairs={{0,1},{1,2},{2,3},{3,4},{4,5},{5,6},{6,7},{7,0},{8,9},{9,10},{10,1... | collective-permute-start | bytes 98312 | tf_op jit(solution)/shard_map/ppermute | solution.py:26
  208.6 4.6 %collective-permute-start.7 = (bf16[128,128]{0,1:T(8,128)(2,1)S(1)}, bf16[128,128]{0,1:T(8,128)(2,1)S(1)}, u32[]{:S(2)}, u32[]{:S(2)}) collective-permute-start(bf16[128,128]{0,1:T(8,128)(2,1)S(1)} %collective-permute-done.6), channel_id=1, source_target_pairs={{1,0},{2,1},{3,2},{4,3},{5,4},{6,5},{7,6},{0,7},{9,8},{10,9},{11,1... | collective-permute-start | bytes 98312 | tf_op jit(solution)/shard_map/ppermute | solution.py:28
  293.0 2.2 slice-start
  293.0 6.1 %copy-start.6 = (f32[16]{0:T(128)S(1)}, f32[16]{0:T(128)}, u32[]{:S(2)}) copy-start(f32[16]{0:T(128)} %param.20) | copy-start | bytes 196
  295.2 4.0 %slice-start.1 = ((bf16[128,1152]{0,1:T(8,128)(2,1)}), bf16[128,1024]{0,1:T(8,128)(2,1)S(1)}, s32[]{:S(2)}) async-start(bf16[128,1152]{0,1:T(8,128)(2,1)} %copy-done), calls=%async_computation.3 | async-start | bytes 524288 | tf_op jit(solution)/shard_map/slice | solution.py:129
Sparse Core Ops, SparseCore 0:
  11.5 166.0 all-gather.2
  214.9 77.0 all-gather.4
